TPU v7x, 256 devices: a whole 4x4x8 slice. The times are simulated.
256 devices in a mesh: row: 8 (over y, core), col: 32 (over z, x).
Axes of the slice: x: 4, y: 4, z: 8, core: 2. Of those that a mesh axis runs over, the one named last changes fastest.
Arguments:
- blocks: float32 [128, 32, 256, 256], P('row', 'col'), may hold values from -6 to 6
- panel_rows: int32 [2, 64], P(None, 'row'), may hold values from -1 to 767, as said below
- target_slots: int32 [2, 128, 32], P(None, 'row', 'col'), may hold values from -1 to 7, as said below
- diag_inverse: float32 [2, 256, 256], replicated, may hold values from -1 to 1, as said below
- cross_block: float32 [256, 256], replicated, may hold values from -6 to 6
Outputs:
- factored: float32 [128, 32, 256, 256], P('row', 'col')
Inputs may be any that keep to these rules, and one draw needn't show every extreme that they name: `panel_rows`: slot q * 2 + m of row device r stands for the m-th structure row of block column class r + q times the number of row devices; both lists are -1 where that class is 0 or 1, and list 0 is -1 also where block column 0 lacks the row; otherwise list 0 equals list 1. `target_slots`: A filled slot of class c names in entry 0 a slot of its own row device and in entry 1 a slot of row device c modulo the number of row devices, within (c // number of row devices) * 2 and the 1 after it; both are filled or both -1, always -1 in classes 0 and 1; the target's block row number is at least its block column number. `diag_inverse`: each matrix is lower triangular.
All inputs are finite; a program needn't handle non-finite values.
Results may differ from a plain program's by a relative error of at most 0.0003.
Values sent between devices are 32-bit elements; how exact they have to be, the bound alone decides.
No kernel may reach another device: no remote copies, remote signals or barrier semaphores. Data moves between devices by JAX's collectives and lax.ppermute only.
A program may use at most 128 MiB of HBM per device.

v0:
```python
import jax
import jax.numpy as jnp
from jax import lax
from jax.sharding import PartitionSpec as P

PER_CLASS = 2
HIGHEST_PRECISION = lax.Precision.HIGHEST


def broadcast(array, axis, root):
    mine = lax.axis_index(axis) == root
    return lax.psum(jnp.where(mine, array, jnp.zeros_like(array)), axis)


def apply_inverse(panel_rows_block, inverse):
    return jnp.einsum("ab,cb->ac", panel_rows_block, inverse, precision=HIGHEST_PRECISION)


def per_device(blocks, panel_rows, target_slots, diag_inverse, cross_block):
    column = lax.axis_index("col")
    row_count = lax.axis_size("row")
    col_count = lax.axis_size("col")
    stored = blocks[:, 0]
    slot_count = panel_rows.shape[1]
    block = stored.shape[-1]
    head_part = stored[:slot_count]
    chunk = slot_count * block // col_count
    pieces = head_part.reshape(col_count, chunk, block)
    received = lax.all_to_all(pieces, "col", 0, 0, tiled=True)
    zero_rows = received[0]
    one_rows = received[1]
    piece_slot = column * chunk // block
    first_live = lax.dynamic_index_in_dim(panel_rows[0], piece_slot, keepdims=False) >= 0
    second_live = lax.dynamic_index_in_dim(panel_rows[1], piece_slot, keepdims=False) >= 0
    cross_factor = jnp.dot(cross_block, diag_inverse[0].T, precision=HIGHEST_PRECISION)
    first_piece = jnp.where(first_live, apply_inverse(zero_rows, diag_inverse[0]), 0.0)
    updated_piece = one_rows - apply_inverse(first_piece, cross_factor)
    second_piece = jnp.where(second_live, apply_inverse(updated_piece, diag_inverse[1]), 0.0)
    both_pieces = jnp.stack([first_piece, second_piece])
    both_rows = lax.all_gather(both_pieces, "col", axis=1, tiled=True)
    both_rows = both_rows.reshape(2, slot_count, block, block)
    first_rows = both_rows[0]
    second_rows = both_rows[1]
    class_start = column // row_count * PER_CLASS
    owner_row = column % row_count
    both_cols = broadcast(
        lax.dynamic_slice_in_dim(both_rows, class_start, PER_CLASS, 1), "row", owner_row
    )
    first_cols = both_cols[0]
    second_cols = both_cols[1]
    row_index = target_slots[0, :, 0]
    col_index = target_slots[1, :, 0]
    present = row_index >= 0
    left_slot = jnp.where(present, row_index, 0)
    right_slot = jnp.where(present, col_index - class_start, 0)
    left_blocks = jnp.concatenate([first_rows[left_slot], second_rows[left_slot]], axis=2)
    right_blocks = jnp.concatenate([first_cols[right_slot], second_cols[right_slot]], axis=2)
    schur_term = jnp.einsum("sak,sbk->sab", left_blocks, right_blocks, precision=HIGHEST_PRECISION)
    trailing = stored - jnp.where(present[:, None, None], schur_term, 0.0)
    head_live = panel_rows >= 0
    keep_mask = ((column == 0) & head_live[0] | (column == 1) & head_live[1])[:, None, None]
    own_panel = jnp.where(column == 0, first_rows, second_rows)
    head_blocks = jnp.where(keep_mask, own_panel, trailing[:slot_count])
    factored = jnp.concatenate([head_blocks, trailing[slot_count:]], axis=0)
    return factored[:, None]


def solution(mesh):
    return jax.shard_map(
        per_device,
        mesh=mesh,
        in_specs=(P("row", "col", None, None), P(None, "row"), P(None, "row", "col"), P(), P()),
        out_specs=P("row", "col", None, None),
        check_vma=False,
    )
```

profile of v0, /device:TPU:2, one launch (start us, length us, event | category | flops | bytes accessed | tf_op | source)
XLA Modules:
  0.0 260.4 jit_solution(12338296099703063530)
XLA Ops:
  6.5 3.1 %slice.58 = f32[8,1,256,256]{3,2,1,0:T(8,128)} slice(f32[16,1,256,256]{3,2,1,0:T(8,128)} %param.5), slice={[0:8], [0:1], [0:256], [0:256]} | slice | bytes 4194304 | tf_op jit(solution)/shard_map/slice | solution.py:26
  9.7 11.7 %all-to-all-start = ((f32[32,64,256]{2,1,0:T(8,128)}), f32[32,64,256]{2,1,0:T(8,128)S(1)}, u32[]{:S(2)}, u32[]{:S(2)}) async-start(f32[32,64,256]{2,1,0:T(8,128)} %bitcast.2), calls=%async_computation | async-start | bytes 4194304 | tf_op jit(solution)/shard_map/all_to_all | solution.py:29
  21.4 0.0 all-gather.2.cloned.1.call-start
  21.5 0.7 fusion.24
  22.2 0.4 fusion.13
  22.6 48.0 %all-to-all-done = f32[32,64,256]{2,1,0:T(8,128)S(1)} async-done(((f32[32,64,256]{2,1,0:T(8,128)}), f32[32,64,256]{2,1,0:T(8,128)S(1)}, u32[]{:S(2)}, u32[]{:S(2)}) %all-to-all-start) | async-done | bytes 2097184 | tf_op jit(solution)/shard_map/all_to_all | solution.py:29
  70.7 0.9 convolution_select_fusion.1
  71.6 0.4 convolution_subtract_fusion
  71.9 1.1 fusion.7
  73.0 0.7 pad_maximum_fusion
  73.7 0.0 all-gather.2.cloned.1.call-update
  73.7 0.0 all-reduce.2.cloned.1.call-start
  73.9 78.7 %all-gather.2.cloned.1.call-done = f32[2,2048,256]{2,1,0:T(8,128)} async-done(((f32[2,64,256]{2,1,0:T(8,128)}), f32[2,2048,256]{2,1,0:T(8,128)}) %all-gather.2.cloned.1.call-update) | async-done | bytes 4194320 | tf_op jit(solution)/shard_map/all_gather | solution.py:40
  152.5 2.3 dynamic-slice_select_fusion
  154.8 3.8 %fusion.22 = (f32[1,2048,256]{2,1,0:T(8,128)S(1)}, f32[1,2048,256]{2,1,0:T(8,128)}) fusion(f32[2,2048,256]{2,1,0:T(8,128)} %all-gather.2.cloned.1.call-done), kind=kLoop, calls=%fused_computation.45 | loop fusion | bytes 8388608 | tf_op jit(solution)/shard_map/slice | solution.py:42
  158.7 2.8 %gather_fusion = f32[16,256,256]{2,1,0:T(8,128)} fusion(f32[8,256,256]{2,1,0:T(8,128)S(1)} %bitcast.55, s32[1024]{0:T(1024)S(1)} %get-tuple-element.18), kind=kCustom, calls=%fused_computation | custom fusion | bytes 8388672 | tf_op jit(solution)/shard_map/gather | solution.py:56
  161.5 4.4 %gather_fusion.1 = f32[16,256,256]{2,1,0:T(8,128)} fusion(f32[8,256,256]{2,1,0:T(8,128)} %bitcast.57, s32[1024]{0:T(1024)S(1)} %get-tuple-element.18), kind=kCustom, calls=%fused_computation.1 | custom fusion | bytes 8388672 | tf_op jit(solution)/shard_map/gather | solution.py:56
  165.8 55.4 %all-reduce.2.cloned.1.call-done = f32[2,2,256,256]{3,2,1,0:T(8,128)} async-done(((f32[2,2,256,256]{3,2,1,0:T(8,128)}), f32[2,2,256,256]{3,2,1,0:T(8,128)}) %all-reduce.2.cloned.1.call-update) | async-done | bytes 1048592 | tf_op jit(solution)/shard_map/psum | solution.py:12
  221.2 1.3 slice_bitcast_fusion.1
  222.5 2.8 %gather_fusion.2 = f32[16,256,256]{2,1,0:T(8,128)} fusion(f32[2,256,256]{2,1,0:T(8,128)S(1)} %get-tuple-element.9, s32[1024]{0:T(1024)S(1)} %get-tuple-element.17), kind=kCustom, calls=%fused_computation.2 | custom fusion | bytes 8388672 | tf_op jit(solution)/shard_map/gather | solution.py:57
  225.2 2.8 %gather_fusion.3 = f32[16,256,256]{2,1,0:T(8,128)} fusion(f32[2,256,256]{2,1,0:T(8,128)S(1)} %get-tuple-element.10, s32[1024]{0:T(1024)S(1)} %get-tuple-element.17), kind=kCustom, calls=%fused_computation.3 | custom fusion | bytes 8388672 | tf_op jit(solution)/shard_map/gather | solution.py:57
  228.1 22.4 %bitcast_subtract_fusion = f32[16,256,256]{2,1,0:T(8,128)S(1)} fusion(f32[16,1,256,256]{3,2,1,0:T(8,128)} %param.5, pred[16]{0:T(512)(128)(4,1)S(1)} %compare_bitcast_fusion, f32[16,256,256]{2,1,0:T(8,128)} %gather_fusion.3, f32[16,256,256]{2,1,0:T(8,128)} %gather_fusion.2, f32[16,256,256]{2,1,0:T(8,128)} %gather_fusion.1, f32[16,256,256]{2,1,0:T(8,128)} %gather_fusion), kind=kOutput, calls=%fused_computation.12 | convolution fusion | flops 6448742400 | bytes 25165840 | tf_op jit(solution)/shard_map/sak,sbk->sab/dot_general | solution.py:58
  250.5 0.6 slice_select_fusion
  251.1 2.4 maximum_bitcast_fusion
  (17 shorter events, 0.1 us)
Async XLA Ops:
  6.5 15.6 %copy-start = (f32[256,256]{1,0:T(8,128)S(1)}, f32[256,256]{1,0:T(8,128)}, u32[]{:S(2)}) copy-start(f32[256,256]{1,0:T(8,128)} %param.9) | copy-start | bytes 786436
  6.5 14.9 %copy-start.4 = (s32[2,8]{1,0:T(2,128)S(1)}, s32[2,8]{1,0:T(2,128)}, u32[]{:S(2)}) copy-start(s32[2,8]{1,0:T(2,128)} %param.6) | copy-start | bytes 196
  6.5 15.6 %copy-start.2 = (f32[2,256,256]{2,1,0:T(8,128)S(1)}, f32[2,256,256]{2,1,0:T(8,128)}, u32[]{:S(2)}) copy-start(f32[2,256,256]{2,1,0:T(8,128)} %param.8) | copy-start | bytes 1572868
  9.7 64.1 %copy-start.3 = (s32[2,16,1]{1,2,0:T(1,128)S(1)}, s32[2,16,1]{1,2,0:T(1,128)}, u32[]{:S(2)}) copy-start(s32[2,16,1]{1,2,0:T(1,128)} %param.7) | copy-start | bytes 388
  9.7 61.0 %all-to-all-start = ((f32[32,64,256]{2,1,0:T(8,128)}), f32[32,64,256]{2,1,0:T(8,128)S(1)}, u32[]{:S(2)}, u32[]{:S(2)}) async-start(f32[32,64,256]{2,1,0:T(8,128)} %bitcast.2), calls=%async_computation | async-start | bytes 4194304 | tf_op jit(solution)/shard_map/all_to_all | solution.py:29
  21.4 131.1 %all-gather.2.cloned.1.call-start = ((), (), s32[]{:S(2)}) async-start(), calls=%async_computation.1 | async-start | bytes 4325376 | tf_op jit(solution)/shard_map/all_gather | solution.py:40
  73.7 147.5 %all-reduce.2.cloned.1.call-start = ((), (), s32[]{:S(2)}) async-start(), calls=%async_computation.2 | async-start | bytes 2097152 | tf_op jit(solution)/shard_map/psum | solution.py:12
  228.1 22.5 %copy-start.1 = (f32[1,2048,256]{2,1,0:T(8,128)S(1)}, f32[1,2048,256]{2,1,0:T(8,128)}, u32[]{:S(2)}) copy-start(f32[1,2048,256]{2,1,0:T(8,128)} %get-tuple-element.8) | copy-start | bytes 6291460
Sparse Core Ops, SparseCore 0:
  73.8 78.6 all-gather.1
  154.9 66.1 all-reduce.1
where the time goes:
time: 261 us; the launch traced here: 260 us
  waiting for transfers between devices  182 us (70%)
  matrix products  25.2 us (10%)
  local copies, waits for them, and re-layouts  21 us (8%)
  between operations  13.6 us (5%)
  starting transfers between devices  11.8 us (5%)
  other arithmetic  6.69 us (3%)
    all_gather x1, waiting for transfers between devices, per_device(): both_rows = lax.all_gather(both_pieces, 'col', axis=1, tiled=True)  78.7 us
    psum x1, waiting for transfers between devices, broadcast(): return lax.psum(jnp.where(mine, array, jnp.zeros_like(array)), axis)  55.4 us
    all_to_all x1, waiting for transfers between devices, per_device(): received = lax.all_to_all(pieces, 'col', 0, 0, tiled=True)  48 us
    dot_general x1, matrix products, per_device(): jnp.einsum('sak,sbk->sab', left_blocks, right_blocks, precision=HIGHEST_P...  22.4 us
    all_to_all x1, starting transfers between devices, per_device(): received = lax.all_to_all(pieces, 'col', 0, 0, tiled=True)  11.7 us
  transfers between devices with their start and end apart: 3, of which 3 were waited for; matrix products, arithmetic and copies ran while one was open for 5% of the time, Pallas kernels for 0%

commit v1 on v0

--- a/solution.py
+++ b/solution.py
@@ -37,7 +37,9 @@
     updated_piece = one_rows - apply_inverse(first_piece, cross_factor)
     second_piece = jnp.where(second_live, apply_inverse(updated_piece, diag_inverse[1]), 0.0)
     both_pieces = jnp.stack([first_piece, second_piece])
-    both_rows = lax.all_gather(both_pieces, "col", axis=1, tiled=True)
+    both_rows = jnp.concatenate(
+        lax.all_to_all(jnp.stack([both_pieces] * lax.axis_size("col")), "col", 0, 0), axis=1
+    )
     both_rows = both_rows.reshape(2, slot_count, block, block)
     first_rows = both_rows[0]
     second_rows = both_rows[1]

time: 261 us -> 287 us (1.100)
  waiting for transfers between devices: 182 us -> 196 us
  local copies, waits for them, and re-layouts: 21 us -> 28.2 us
  starting transfers between devices: 11.8 us -> 18.9 us
    all_to_all x0 -> x1, waiting for transfers between devices: none -> 91.5 us  [per_device(): lax.all_to_all(jnp.stack([both_pieces] * lax.axis_size('col')), 'col', 0, 0)]
    all_gather x1 -> x0, waiting for transfers between devices: 78.7 us -> none  [per_device(): both_rows = lax.all_gather(both_pieces, 'col', axis=1, tiled=True)]
    all_to_all x0 -> x1, starting transfers between devices: none -> 7.05 us  [per_device(): lax.all_to_all(jnp.stack([both_pieces] * lax.axis_size('col')), 'col', 0, 0)]
  transfers between devices with their start and end apart: 3 -> 3, of which waited for: 3 -> 3; matrix products, arithmetic and copies ran while one was open for 5% -> 4% of each run, Pallas kernels for 0% -> 0%
where the time goes in v1:
time: 287 us
  waiting for transfers between devices  196 us (68%)
  local copies, waits for them, and re-layouts  28.2 us (10%)
  matrix products  25.2 us (9%)
  starting transfers between devices  18.9 us (7%)
  between operations  13.6 us (5%)
  other arithmetic  4.81 us (2%)
    all_to_all x1, waiting for transfers between devices, per_device(): lax.all_to_all(jnp.stack([both_pieces] * lax.axis_size('col')), 'col', 0, 0)  91.5 us
    psum x1, waiting for transfers between devices, broadcast(): return lax.psum(jnp.where(mine, array, jnp.zeros_like(array)), axis)  56.5 us
    all_to_all x1, waiting for transfers between devices, per_device(): received = lax.all_to_all(pieces, 'col', 0, 0, tiled=True)  48.1 us
    dot_general x1, matrix products, per_device(): jnp.einsum('sak,sbk->sab', left_blocks, right_blocks, precision=HIGHEST_P...  22.4 us
    all_to_all x1, starting transfers between devices, per_device(): received = lax.all_to_all(pieces, 'col', 0, 0, tiled=True)  11.6 us
    all_to_all x1, starting transfers between devices, per_device(): lax.all_to_all(jnp.stack([both_pieces] * lax.axis_size('col')), 'col', 0, 0)  7.05 us
  transfers between devices with their start and end apart: 3, of which 3 were waited for; matrix products, arithmetic and copies ran while one was open for 4% of the time, Pallas kernels for 0%

profile of v1, /device:TPU:2, one launch (start us, length us, event | category | flops | bytes accessed | tf_op | source)
XLA Modules:
  0.0 286.8 jit_solution(13020527015502377754)
XLA Ops:
  6.5 3.1 %slice.58 = f32[8,1,256,256]{3,2,1,0:T(8,128)} slice(f32[16,1,256,256]{3,2,1,0:T(8,128)} %param.5), slice={[0:8], [0:1], [0:256], [0:256]} | slice | bytes 4194304 | tf_op jit(solution)/shard_map/slice | solution.py:26
  9.7 11.6 %all-to-all-start = ((f32[32,64,256]{2,1,0:T(8,128)}), f32[32,64,256]{2,1,0:T(8,128)S(1)}, u32[]{:S(2)}, u32[]{:S(2)}) async-start(f32[32,64,256]{2,1,0:T(8,128)} %bitcast.2), calls=%async_computation | async-start | bytes 4194304 | tf_op jit(solution)/shard_map/all_to_all | solution.py:29
  21.3 0.7 fusion.24
  22.0 0.4 fusion.13
  22.4 48.1 %all-to-all-done = f32[32,64,256]{2,1,0:T(8,128)S(1)} async-done(((f32[32,64,256]{2,1,0:T(8,128)}), f32[32,64,256]{2,1,0:T(8,128)S(1)}, u32[]{:S(2)}, u32[]{:S(2)}) %all-to-all-start) | async-done | bytes 2097184 | tf_op jit(solution)/shard_map/all_to_all | solution.py:29
  70.5 0.9 convolution_select_fusion.1
  71.4 0.4 convolution_subtract_fusion
  71.8 1.1 fusion.7
  72.9 2.5 stack.11
  75.4 7.0 %all-to-all-start.1 = ((f32[32,2,64,256]{3,2,1,0:T(8,128)}), f32[32,2,64,256]{3,2,1,0:T(8,128)}, u32[]{:S(2)}, u32[]{:S(2)}) async-start(f32[32,2,64,256]{3,2,1,0:T(8,128)} %stack.11), calls=%async_computation.1 | async-start | bytes 8388608 | tf_op jit(solution)/shard_map/all_to_all | solution.py:41
  82.8 91.5 %all-to-all-done.1 = f32[32,2,64,256]{3,2,1,0:T(8,128)} async-done(((f32[32,2,64,256]{3,2,1,0:T(8,128)}), f32[32,2,64,256]{3,2,1,0:T(8,128)}, u32[]{:S(2)}, u32[]{:S(2)}) %all-to-all-start.1) | async-done | bytes 4194336 | tf_op jit(solution)/shard_map/all_to_all | solution.py:41
  174.3 2.5 copy.12
  176.8 2.0 copy-done.2
  178.8 1.1 dynamic-slice_select_fusion
  179.9 4.0 %fusion.22 = (f32[1,32,64,256]{3,2,1,0:T(8,128)S(1)}, f32[1,32,64,256]{3,2,1,0:T(8,128)}) fusion(f32[2,32,64,256]{3,2,1,0:T(8,128)} %bitcast.64), kind=kLoop, calls=%fused_computation.46 | loop fusion | bytes 8388608 | tf_op jit(solution)/shard_map/slice | solution.py:44
  183.9 2.8 gather_fusion
  186.7 4.4 %gather_fusion.1 = f32[16,256,256]{2,1,0:T(8,128)} fusion(f32[8,256,256]{2,1,0:T(8,128)} %bitcast.61, s32[1024]{0:T(1024)S(1)} %get-tuple-element.20), kind=kCustom, calls=%fused_computation.1 | custom fusion | bytes 8388672 | tf_op jit(solution)/shard_map/gather | solution.py:58
  191.1 56.5 %all-reduce.2.cloned.1.call-done = f32[2,2,256,256]{3,2,1,0:T(8,128)} async-done(((f32[2,2,256,256]{3,2,1,0:T(8,128)}), f32[2,2,256,256]{3,2,1,0:T(8,128)}) %all-reduce.2.cloned.1.call-update) | async-done | bytes 1048592 | tf_op jit(solution)/shard_map/psum | solution.py:12
  247.5 1.3 slice_bitcast_fusion.1
  248.8 2.8 gather_fusion.2
  251.6 2.8 gather_fusion.3
  254.4 22.4 %bitcast_subtract_fusion = f32[16,256,256]{2,1,0:T(8,128)S(1)} fusion(f32[16,1,256,256]{3,2,1,0:T(8,128)} %param.5, pred[16]{0:T(512)(128)(4,1)S(1)} %compare_bitcast_fusion, f32[16,256,256]{2,1,0:T(8,128)} %gather_fusion.3, f32[16,256,256]{2,1,0:T(8,128)} %gather_fusion.2, f32[16,256,256]{2,1,0:T(8,128)} %gather_fusion.1, f32[16,256,256]{2,1,0:T(8,128)} %gather_fusion), kind=kOutput, calls=%fused_computation.12 | convolution fusion | flops 6448742400 | bytes 25165840 | tf_op jit(solution)/shard_map/sak,sbk->sab/dot_general | solution.py:60
  276.9 0.6 slice_select_fusion
  277.5 2.4 maximum_bitcast_fusion
  (20 shorter events, 0.3 us)
Async XLA Ops:
  6.5 15.5 %copy-start = (f32[256,256]{1,0:T(8,128)S(1)}, f32[256,256]{1,0:T(8,128)}, u32[]{:S(2)}) copy-start(f32[256,256]{1,0:T(8,128)} %param.9) | copy-start | bytes 786436
  6.5 14.8 %copy-start.5 = (s32[2,8]{1,0:T(2,128)S(1)}, s32[2,8]{1,0:T(2,128)}, u32[]{:S(2)}) copy-start(s32[2,8]{1,0:T(2,128)} %param.6) | copy-start | bytes 196
  6.5 15.5 %copy-start.3 = (f32[2,256,256]{2,1,0:T(8,128)S(1)}, f32[2,256,256]{2,1,0:T(8,128)}, u32[]{:S(2)}) copy-start(f32[2,256,256]{2,1,0:T(8,128)} %param.8) | copy-start | bytes 1572868
  9.7 60.9 %all-to-all-start = ((f32[32,64,256]{2,1,0:T(8,128)}), f32[32,64,256]{2,1,0:T(8,128)S(1)}, u32[]{:S(2)}, u32[]{:S(2)}) async-start(f32[32,64,256]{2,1,0:T(8,128)} %bitcast.2), calls=%async_computation | async-start | bytes 4194304 | tf_op jit(solution)/shard_map/all_to_all | solution.py:29
  75.4 7.3 %copy-start.4 = (s32[2,16,1]{1,2,0:T(1,128)S(1)}, s32[2,16,1]{1,2,0:T(1,128)}, u32[]{:S(2)}) copy-start(s32[2,16,1]{1,2,0:T(1,128)} %param.7) | copy-start | bytes 388
  75.4 98.9 %all-to-all-start.1 = ((f32[32,2,64,256]{3,2,1,0:T(8,128)}), f32[32,2,64,256]{3,2,1,0:T(8,128)}, u32[]{:S(2)}, u32[]{:S(2)}) async-start(f32[32,2,64,256]{3,2,1,0:T(8,128)} %stack.11), calls=%async_computation.1 | async-start | bytes 8388608 | tf_op jit(solution)/shard_map/all_to_all | solution.py:41
  82.5 165.1 %all-reduce.2.cloned.1.call-start = ((), (), s32[]{:S(2)}) async-start(), calls=%async_computation.2 | async-start | bytes 2097152 | tf_op jit(solution)/shard_map/psum | solution.py:12
  176.8 2.0 copy-start.2
  254.4 22.5 %copy-start.1 = (f32[1,32,64,256]{3,2,1,0:T(8,128)S(1)}, f32[1,32,64,256]{3,2,1,0:T(8,128)}, u32[]{:S(2)}) copy-start(f32[1,32,64,256]{3,2,1,0:T(8,128)} %get-tuple-element.8) | copy-start | bytes 6291460
Sparse Core Ops, SparseCore 0:
  180.0 67.4 all-reduce.1
